TPU v7x, 32 devices: a whole 2x2x4 slice. The times are simulated.
32 devices in a mesh: req: 2 (over x), ctx: 8 (over z, core), exp: 2 (over y).
Axes of the slice: x: 2, y: 2, z: 4, core: 2. Of those that a mesh axis runs over, the one named last changes fastest.
Arguments:
- query_states: bfloat16 [2, 512, 1024], P('req', 'ctx', 'exp'), may hold values from -6 to 6
- key_states: bfloat16 [2, 512, 1024], P('req', 'ctx', 'exp'), may hold values from -6 to 6
- value_states: bfloat16 [2, 512, 1024], P('req', 'ctx', 'exp'), may hold values from -6 to 6
- residual: bfloat16 [2, 512, 2048], P('req', ('ctx', 'exp')), may hold values from -6 to 6
- out_weight: bfloat16 [2048, 1024], P('ctx', 'exp'), may hold values from -0.1875 to 0.1875
- norm_gain: float32 [2048], replicated, may hold values from 0.1 to 1.9
- gate_weight: bfloat16 [8, 2048, 704], P('ctx', None, 'exp'), may hold values from -0.125 to 0.125
- up_weight: bfloat16 [8, 2048, 704], P('ctx', None, 'exp'), may hold values from -0.125 to 0.125
- down_weight: bfloat16 [8, 704, 2048], P('ctx', 'exp'), may hold values from -0.21875 to 0.21875
- routes: int32 [2, 512, 4], P('req', 'ctx'), may hold values from 0 to 7, all different within a row; in each aligned block of 64 rows (0 to 63, 64 to 127, ..., all dimensions but the last counted through in order) at most 48 rows name the same one
- route_weights: float32 [2, 512, 4], P('req', 'ctx'), may hold values from 0.1 to 1
- prompt_lengths: int32 [2], P('req'), may hold values from 128 to 512, as said below
Outputs:
- layer_out: bfloat16 [2, 512, 2048], P('req', ('ctx', 'exp'))
- cache_keys: bfloat16 [2, 512, 1024], P('req', 'ctx', 'exp')
- cache_values: bfloat16 [2, 512, 1024], P('req', 'ctx', 'exp')
Inputs may be any that keep to these rules, and one draw needn't show every extreme that they name: `routes`: each row names 4 different experts; in each aligned block of 64 rows of a request no expert is named by more than 48 rows, a bound that some block reaches. `prompt_lengths`: one request has exactly 512 tokens.
All inputs are finite; a program needn't handle non-finite values.
Results may differ from a plain program's by a relative error of at most 0.019.
Values may be sent and summed in bfloat16 or wider, within the bound.
No kernel may reach another device: no remote copies, remote signals or barrier semaphores. Data moves between devices by JAX's collectives and lax.ppermute only.
A program may use at most 64 MiB of HBM per device.

v0:
```python
import jax
import jax.numpy as jnp
from jax import lax
from jax.sharding import PartitionSpec as P

D = 2048
HD = 128
TOP = 4
EPS = 1e-06
NEG = -1e30


def row_positions(row_ids, half_block, n_groups):
    block_ids = row_ids // half_block
    device = block_ids // 2
    target = jnp.where(block_ids % 2 == 0, device, 2 * n_groups - 1 - device)
    return target * half_block + row_ids % half_block


def slot_tables(route_block, weight_block, experts, capacity):
    tok_here, top_here = route_block.shape
    flat_ids = route_block.reshape(tok_here * top_here)
    hit_table = (flat_ids[:, None] == jnp.arange(experts, dtype=jnp.int32)[None, :]).astype(
        jnp.int32
    )
    before = jnp.cumsum(hit_table, axis=0) - hit_table
    slot_rank = jnp.sum(before * hit_table, axis=1)
    slot_index = flat_ids * capacity + slot_rank
    slot_match = (
        jnp.arange(experts * capacity, dtype=jnp.int32)[:, None] == slot_index[None, :]
    ).astype(jnp.float32)
    slot_match = slot_match.reshape(experts * capacity, tok_here, top_here)
    dispatch = jnp.sum(slot_match, axis=2)
    combine = jnp.transpose(jnp.sum(slot_match * weight_block[None, :, :], axis=2))
    return (dispatch, combine)


def expert_ffn(token_rows, gate_matrix, up_matrix, down_matrix):
    gate_act = jnp.dot(token_rows, gate_matrix, preferred_element_type=jnp.float32)
    up_act = jnp.dot(token_rows, up_matrix, preferred_element_type=jnp.float32)
    hidden = (jax.nn.silu(gate_act) * up_act).astype(jnp.bfloat16)
    return jnp.dot(hidden, down_matrix, preferred_element_type=jnp.float32)


def exp_swap(x):
    return lax.ppermute(x, "exp", perm=[(0, 1), (1, 0)])


def exp_reduce_rows(parts):
    if lax.axis_size("exp") != 2:
        return lax.psum_scatter(
            parts.astype(jnp.bfloat16), "exp", scatter_dimension=0, tiled=True
        ).astype(jnp.float32)
    half = parts.shape[0] // 2
    first = lax.axis_index("exp") == 0
    lower = parts[:half]
    upper = parts[half:]
    mine = jnp.where(first, lower, upper)
    theirs = jnp.where(first, upper, lower)
    got = exp_swap(theirs.astype(jnp.bfloat16))
    return mine + got.astype(jnp.float32)


def exp_gather_rows(rows):
    if lax.axis_size("exp") != 2:
        return lax.all_gather(rows, "exp", axis=0, tiled=True)
    got = exp_swap(rows)
    first = lax.axis_index("exp") == 0
    return jnp.where(
        first, jnp.concatenate([rows, got], axis=0), jnp.concatenate([got, rows], axis=0)
    )


def local(
    query_states,
    key_states,
    value_states,
    residual,
    out_weight,
    norm_gain,
    gate_weight,
    up_weight,
    down_weight,
    routes,
    route_weights,
    prompt_lengths,
):
    n_ctx = lax.axis_size("ctx")
    my_ctx = lax.axis_index("ctx")
    tok_here = query_states.shape[1]
    feat_width = query_states.shape[2]
    heads_dev = feat_width // HD
    half_block = tok_here // 2
    score_scale = HD ** (-0.5)
    length = prompt_lengths[0]
    local_ids = jnp.arange(tok_here, dtype=jnp.int32)
    query_pos = row_positions(my_ctx * tok_here + local_ids, half_block, n_ctx)
    decode_pos = my_ctx * tok_here + local_ids
    query_three = query_states[0].reshape(tok_here, heads_dev, HD)
    run_max = jnp.full((heads_dev, tok_here), NEG, jnp.float32)
    kv_here = jnp.concatenate([key_states[0], value_states[0]], axis=1)
    kv_all = lax.all_gather(kv_here, "ctx", axis=0, tiled=True)
    key_two = kv_all[:, :feat_width]
    value_two = kv_all[:, feat_width:]
    row_count = key_two.shape[0]
    key_pos = row_positions(jnp.arange(row_count, dtype=jnp.int32), half_block, n_ctx)
    pick_rows = (decode_pos[:, None] == key_pos[None, :]).astype(jnp.bfloat16)
    kept_keys = jnp.dot(pick_rows, key_two, preferred_element_type=jnp.float32)
    kept_values = jnp.dot(pick_rows, value_two, preferred_element_type=jnp.float32)
    old_max = run_max
    key_heads = key_two.reshape(row_count, heads_dev, HD)
    value_heads = value_two.reshape(row_count, heads_dev, HD)
    logits = (
        jnp.einsum("qhd,khd->hqk", query_three, key_heads, preferred_element_type=jnp.float32)
        * score_scale
    )
    visible = (key_pos[None, :] <= query_pos[:, None]) & (key_pos[None, :] < length)
    logits = jnp.where(visible[None], logits, NEG)
    new_max = jnp.maximum(old_max, jnp.max(logits, axis=2))
    weights = jnp.where(visible[None], jnp.exp(logits - new_max[:, :, None]), 0.0)
    new_sum = jnp.sum(weights, axis=2)
    gained = jnp.einsum(
        "hqk,khd->hqd",
        weights.astype(jnp.bfloat16),
        value_heads,
        preferred_element_type=jnp.float32,
    )
    inner_state = (new_max, new_sum, gained)
    run_max, run_sum, run_out, kept_keys, kept_values = inner_state + (kept_keys, kept_values)
    mixed = (run_out / run_sum[:, :, None]).astype(jnp.bfloat16)
    mixed = jnp.transpose(mixed, (1, 0, 2)).reshape(tok_here, feat_width)
    out_parts = jnp.einsum(
        "tc,oc->to",
        mixed,
        lax.all_gather(out_weight, "ctx", axis=0, tiled=True),
        preferred_element_type=jnp.float32,
    )
    head_total = exp_reduce_rows(out_parts)
    stream = (residual[0].astype(jnp.float32) + head_total).astype(jnp.bfloat16)
    stream_f = stream.astype(jnp.float32)
    mean_sq = jnp.mean(stream_f * stream_f, axis=1, keepdims=True)
    normed = (stream_f * lax.rsqrt(mean_sq + EPS) * norm_gain).astype(jnp.bfloat16)
    all_normed = exp_gather_rows(normed)
    capacity = min(tok_here, 2 * max(1, 3 * tok_here * TOP // (4 * n_ctx)))
    dispatch, combine = slot_tables(routes[0], route_weights[0], n_ctx, capacity)
    send_rows = jnp.dot(
        dispatch.astype(jnp.bfloat16), all_normed, preferred_element_type=jnp.float32
    ).astype(jnp.bfloat16)
    send_rows = send_rows.reshape(n_ctx, capacity, D)
    arrived = lax.all_to_all(send_rows, "ctx", split_axis=0, concat_axis=0, tiled=True)
    slot_count = arrived.shape[1]
    flat_rows = arrived.reshape(n_ctx * slot_count, D)
    produced = expert_ffn(flat_rows, gate_weight[0], up_weight[0], down_weight[0]).reshape(
        n_ctx, slot_count, D
    )
    served = lax.all_to_all(
        produced.astype(jnp.bfloat16), "ctx", split_axis=0, concat_axis=0, tiled=True
    ).astype(produced.dtype)
    results = served.reshape(n_ctx * capacity, D)
    moe_part = jnp.dot(
        combine, results, precision=lax.Precision.HIGHEST, preferred_element_type=jnp.float32
    )
    moe_rows = exp_reduce_rows(moe_part)
    layer_out = (stream.astype(jnp.float32) + moe_rows).astype(jnp.bfloat16)
    return (
        layer_out[None],
        kept_keys.astype(jnp.bfloat16)[None],
        kept_values.astype(jnp.bfloat16)[None],
    )


def solution(mesh):
    return jax.shard_map(
        local,
        mesh=mesh,
        in_specs=(
            P("req", "ctx", "exp"),
            P("req", "ctx", "exp"),
            P("req", "ctx", "exp"),
            P("req", ("ctx", "exp"), None),
            P("ctx", "exp"),
            P(),
            P("ctx", None, "exp"),
            P("ctx", None, "exp"),
            P("ctx", "exp", None),
            P("req", "ctx", None),
            P("req", "ctx", None),
            P("req"),
        ),
        out_specs=(P("req", ("ctx", "exp"), None), P("req", "ctx", "exp"), P("req", "ctx", "exp")),
        check_vma=False,
    )
```

profile of v0, /device:TPU:0, one launch (start us, length us, event | category | flops | bytes accessed | tf_op | source)
XLA Modules:
  0.0 180.0 jit_solution(15707757264715683724)
XLA Ops:
  7.2 1.6 pad_maximum_fusion
  8.9 0.7 all-gather.5.cloned.1.call-update
  10.3 0.8 copy.47
  11.8 0.9 reshape_squeeze.4
  12.8 22.2 %all-gather.3.cloned.1.call-done = bf16[512,1024]{1,0:T(8,128)(2,1)} async-done(((bf16[64,1024]{1,0:T(8,128)(2,1)}), bf16[512,1024]{1,0:T(8,128)(2,1)}) %all-gather.3.cloned.1.call-update) | async-done | bytes 1048592 | tf_op jit(solution)/shard_map/all_gather | solution.py:102
  35.0 1.3 fusion.71
  37.7 27.7 %all-gather.5.cloned.1.call-done = bf16[2048,512]{1,0:T(8,128)(2,1)} async-done(((bf16[256,512]{1,0:T(8,128)(2,1)}), bf16[2048,512]{1,0:T(8,128)(2,1)}) %all-gather.5.cloned.1.call-update) | async-done | bytes 2097168 | tf_op jit(solution)/shard_map/all_gather | solution.py:135
  65.4 2.3 %fusion.38 = f32[64,2048]{1,0:T(8,128)S(1)} fusion(bf16[2048,512]{1,0:T(8,128)(2,1)} %all-gather.5.cloned.1.call-done, bf16[4,8,8,128]{3,2,1,0:T(8,128)(2,1)S(1)} %fusion.15), kind=kOutput, calls=%fused_computation.52 | convolution fusion | flops 134217728 | bytes 2686976 | tf_op jit(solution)/shard_map/tc,oc->to/dot_general | solution.py:132
  67.8 1.5 collective-permute-start
  69.9 3.6 %collective-permute-done = bf16[32,2048]{1,0:T(8,128)(2,1)S(1)} collective-permute-done((bf16[32,2048]{1,0:T(8,128)(2,1)S(1)}, bf16[32,2048]{1,0:T(8,128)(2,1)S(1)}, u32[]{:S(2)}, u32[]{:S(2)}) %collective-permute-start) | collective-permute-done | bytes 131104 | tf_op jit(solution)/shard_map/ppermute | solution.py:46
  73.8 1.5 collective-permute-start.1
  75.6 3.3 %collective-permute-done.1 = bf16[32,2048]{1,0:T(8,128)(2,1)S(1)} collective-permute-done((bf16[32,2048]{1,0:T(8,128)(2,1)S(1)}, bf16[32,2048]{1,0:T(8,128)(2,1)S(1)}, u32[]{:S(2)}, u32[]{:S(2)}) %collective-permute-start.1) | collective-permute-done | bytes 131104 | tf_op jit(solution)/shard_map/ppermute | solution.py:46
  79.4 41.0 %all_to_all.10 = bf16[8,48,2048]{2,1,0:T(8,128)(2,1)S(1)} all-to-all(bf16[8,48,2048]{2,1,0:T(8,128)(2,1)S(1)} %bitcast.73), channel_id=1, replica_groups=mesh['req'=2,'ctx'=8,'exp'=2] {'ctx'}, dimensions={0} | all-to-all | bytes 3145728 | tf_op jit(solution)/shard_map/all_to_all | solution.py:150
  120.4 0.9 fusion.3
  121.8 0.9 fusion.10
  122.9 2.1 %convolution_convert_fusion = bf16[8,48,2048]{2,1,0:T(8,128)(2,1)} fusion(bf16[8,48,352]{2,1,0:T(8,128)(2,1)S(1)} %bitcast.77, bf16[1,352,2048]{2,1,0:T(8,128)(2,1)S(1)} %copy-done), kind=kOutput, calls=%fused_computation | convolution fusion | flops 554434560 | bytes 3284992 | tf_op jit(solution)/shard_map/dot_general | solution.py:42
  125.1 3.6 %all-to-all-start.1 = ((bf16[8,48,2048]{2,1,0:T(8,128)(2,1)}), bf16[8,48,2048]{2,1,0:T(8,128)(2,1)S(1)}, u32[]{:S(2)}, u32[]{:S(2)}) async-start(bf16[8,48,2048]{2,1,0:T(8,128)(2,1)} %convolution_convert_fusion), calls=%async_computation.1 | async-start | bytes 3145728 | tf_op jit(solution)/shard_map/all_to_all | solution.py:156
  128.7 1.9 %fusion.17 = bf16[1,64,512]{2,1,0:T(8,128)(2,1)} fusion(s32[512]{0:T(512)S(1)} %fusion.56, s32[64]{0:T(128)S(1)} %iota_add_fusion, bf16[512,1024]{1,0:T(8,128)(2,1)} %all-gather.3.cloned.1.call-done), kind=kOutput, calls=%fused_computation.19 | convolution fusion | flops 33619968 | bytes 592128 | tf_op jit(solution)/shard_map/dot_general | solution.py:109
  130.6 35.8 %all-to-all-done.1 = bf16[8,48,2048]{2,1,0:T(8,128)(2,1)S(1)} async-done(((bf16[8,48,2048]{2,1,0:T(8,128)(2,1)}), bf16[8,48,2048]{2,1,0:T(8,128)(2,1)S(1)}, u32[]{:S(2)}, u32[]{:S(2)}) %all-to-all-start.1) | async-done | bytes 1572896 | tf_op jit(solution)/shard_map/all_to_all | solution.py:156
  166.4 0.9 fusion.73
  167.3 1.5 collective-permute-start.2
  168.8 0.9 fusion.16
  169.7 2.7 %collective-permute-done.2 = bf16[32,2048]{1,0:T(8,128)(2,1)S(1)} collective-permute-done((bf16[32,2048]{1,0:T(8,128)(2,1)S(1)}, bf16[32,2048]{1,0:T(8,128)(2,1)S(1)}, u32[]{:S(2)}, u32[]{:S(2)}) %collective-permute-start.2) | collective-permute-done | bytes 131104 | tf_op jit(solution)/shard_map/ppermute | solution.py:46
  172.4 0.7 fusion.37
  (47 shorter events, 4.6 us)
Async XLA Ops:
  7.2 115.8 %copy-start = (bf16[1,352,2048]{2,1,0:T(8,128)(2,1)S(1)}, bf16[1,352,2048]{2,1,0:T(8,128)(2,1)}, u32[]{:S(2)}) copy-start(bf16[1,352,2048]{2,1,0:T(8,128)(2,1)} %param.20) | copy-start | bytes 4325380
  7.2 27.9 %all-gather.3.cloned.1.call-start = ((), (), s32[]{:S(2)}) async-start(), calls=%async_computation.2 | async-start | bytes 1179648 | tf_op jit(solution)/shard_map/all_gather | solution.py:102
  8.9 56.5 %all-gather.5.cloned.1.call-start = ((), (), s32[]{:S(2)}) async-start(), calls=%async_computation.3 | async-start | bytes 2359296 | tf_op jit(solution)/shard_map/all_gather | solution.py:135
  37.7 35.8 %copy-start.2 = (bf16[1,32,2048]{2,1,0:T(8,128)(2,1)S(1)}, bf16[1,32,2048]{2,1,0:T(8,128)(2,1)}, u32[]{:S(2)}) copy-start(bf16[1,32,2048]{2,1,0:T(8,128)(2,1)} %param.15) | copy-start | bytes 393220
  37.7 36.0 %copy-start.3 = (f32[2048]{0:T(1024)S(1)}, f32[2048]{0:T(1024)}, u32[]{:S(2)}) copy-start(f32[2048]{0:T(1024)} %param.17) | copy-start | bytes 24580
  67.7 7.7 %copy-start.4 = (f32[1,64,4]{1,2,0:T(4,128)S(1)}, f32[1,64,4]{1,2,0:T(4,128)}, u32[]{:S(2)}) copy-start(f32[1,64,4]{1,2,0:T(4,128)} %param.22) | copy-start | bytes 3076
  67.8 5.7 %collective-permute-start = (bf16[32,2048]{1,0:T(8,128)(2,1)S(1)}, bf16[32,2048]{1,0:T(8,128)(2,1)S(1)}, u32[]{:S(2)}, u32[]{:S(2)}) collective-permute-start(bf16[32,2048]{1,0:T(8,128)(2,1)S(1)} %select_convert_fusion.1), channel_id=1, source_target_pairs={{0,1},{1,0},{2,3},{3,2},{4,5},{5,4},{6,7},{7,6},{8,9},{9,8},{10,11... | collective-permute-start | bytes 393224 | tf_op jit(solution)/shard_map/ppermute | solution.py:46
  73.8 5.0 %collective-permute-start.1 = (bf16[32,2048]{1,0:T(8,128)(2,1)S(1)}, bf16[32,2048]{1,0:T(8,128)(2,1)S(1)}, u32[]{:S(2)}, u32[]{:S(2)}) collective-permute-start(bf16[32,2048]{1,0:T(8,128)(2,1)S(1)} %fusion.22), channel_id=1, source_target_pairs={{0,1},{1,0},{2,3},{3,2},{4,5},{5,4},{6,7},{7,6},{8,9},{9,8},{10,11... | collective-permute-start | bytes 393224 | tf_op jit(solution)/shard_map/ppermute | solution.py:46
  79.4 41.0 %copy-start.5 = (bf16[1,2048,352]{1,2,0:T(8,128)(2,1)S(1)}, bf16[1,2048,352]{1,2,0:T(8,128)(2,1)}, u32[]{:S(2)}) copy-start(bf16[1,2048,352]{1,2,0:T(8,128)(2,1)} %param.18) | copy-start | bytes 4325380
  120.4 1.4 copy-start.6
  125.1 41.3 %all-to-all-start.1 = ((bf16[8,48,2048]{2,1,0:T(8,128)(2,1)}), bf16[8,48,2048]{2,1,0:T(8,128)(2,1)S(1)}, u32[]{:S(2)}, u32[]{:S(2)}) async-start(bf16[8,48,2048]{2,1,0:T(8,128)(2,1)} %convolution_convert_fusion), calls=%async_computation.1 | async-start | bytes 3145728 | tf_op jit(solution)/shard_map/all_to_all | solution.py:156
  166.4 2.4 %copy-start.1 = (bf16[512,1024]{1,0:T(8,128)(2,1)S(1)}, bf16[512,1024]{1,0:T(8,128)(2,1)}, u32[]{:S(2)}) copy-start(bf16[512,1024]{1,0:T(8,128)(2,1)} %all-gather.3.cloned.1.call-done) | copy-start | bytes 3145732
  167.3 5.1 %collective-permute-start.2 = (bf16[32,2048]{1,0:T(8,128)(2,1)S(1)}, bf16[32,2048]{1,0:T(8,128)(2,1)S(1)}, u32[]{:S(2)}, u32[]{:S(2)}) collective-permute-start(bf16[32,2048]{1,0:T(8,128)(2,1)S(1)} %select_convert_fusion), channel_id=1, source_target_pairs={{0,1},{1,0},{2,3},{3,2},{4,5},{5,4},{6,7},{7,6},{8,9},{9,8},{10,11... | collective-permute-start | bytes 393224 | tf_op jit(solution)/shard_map/ppermute | solution.py:46
Sparse Core Ops, SparseCore 0:
  10.2 24.8 all-gather.2
  36.6 28.7 all-gather.4
where the time goes:
time: 180 us
  waiting for transfers between devices  96.1 us (53%)
  blocking collectives  41 us (23%)
  between operations  14.9 us (8%)
  matrix products  11.2 us (6%)
  starting transfers between devices  8.24 us (5%)
  local copies, waits for them, and re-layouts  4.62 us (3%)
  other arithmetic  3.95 us (2%)
    all_to_all x1, blocking collectives, local(): lax.all_to_all(send_rows, 'ctx', split_axis=0, concat_axis=0, tiled=True)  41 us
    all_to_all x1, waiting for transfers between devices, local(): lax.all_to_all(produced.astype(jnp.bfloat16), 'ctx', split_axis=0, concat...  35.8 us
    all_gather x1, waiting for transfers between devices, local(): lax.all_gather(out_weight, 'ctx', axis=0, tiled=True)  27.7 us
    all_gather x1, waiting for transfers between devices, local(): kv_all = lax.all_gather(kv_here, 'ctx', axis=0, tiled=True)  22.2 us
    ppermute x3, waiting for transfers between devices, exp_swap(): return lax.ppermute(x, 'exp', perm=[(0, 1), (1, 0)])  9.58 us
    ppermute x3, starting transfers between devices, exp_swap(): return lax.ppermute(x, 'exp', perm=[(0, 1), (1, 0)])  4.58 us
  transfers between devices with their start and end apart: 6, of which 6 were waited for; matrix products, arithmetic and copies ran while one was open for 5% of the time, Pallas kernels for 0%

commit v1 on v0

--- a/solution.py
+++ b/solution.py
@@ -8,6 +8,27 @@
 TOP = 4
 EPS = 1e-06
 NEG = -1e30
+
+
+def domain_answer(piece_in, out_dim):
+    row_out = list(piece_in.shape[1:])
+    row_out[out_dim] *= piece_in.shape[0]
+    return jnp.moveaxis(piece_in, 0, out_dim).reshape(row_out)
+
+
+def _recast_ticks(array_here, axis_id):
+    inter, opened = (lax.axis_size(axis_id), lax.axis_index(axis_id))
+    base_arr, shaped = (array_here[None], 1)
+    while shaped < inter:
+        oldest = lax.ppermute(
+            base_arr, axis_name=axis_id, perm=tuple(((k0, k0 ^ shaped) for k0 in range(inter)))
+        )
+        v_now = opened & shaped == 0
+        base_arr = jnp.concatenate(
+            [jnp.where(v_now, base_arr, oldest), jnp.where(v_now, oldest, base_arr)]
+        )
+        shaped *= 2
+    return base_arr
 
 
 def row_positions(row_ids, half_block, n_groups):
@@ -99,7 +120,7 @@
     query_three = query_states[0].reshape(tok_here, heads_dev, HD)
     run_max = jnp.full((heads_dev, tok_here), NEG, jnp.float32)
     kv_here = jnp.concatenate([key_states[0], value_states[0]], axis=1)
-    kv_all = lax.all_gather(kv_here, "ctx", axis=0, tiled=True)
+    kv_all = domain_answer(_recast_ticks(kv_here, "ctx"), 0)
     key_two = kv_all[:, :feat_width]
     value_two = kv_all[:, feat_width:]
     row_count = key_two.shape[0]

time: 180 us -> 180 us (level)
  starting transfers between devices: 8.24 us -> 14.5 us
  waiting for transfers between devices: 96.1 us -> 90.9 us
    ppermute x0 -> x3, waiting for transfers between devices: none -> 45.1 us  [_recast_ticks(): lax.ppermute(base_arr, axis_name=axis_id, perm=tuple(((k0, k0 ^ shaped) f...]
    all_gather x1, waiting for transfers between devices: 27.7 us -> 0.02 us  [local(): lax.all_gather(out_weight, 'ctx', axis=0, tiled=True)]
    all_gather x1 -> x0, waiting for transfers between devices: 22.2 us -> none  [local(): kv_all = lax.all_gather(kv_here, 'ctx', axis=0, tiled=True)]
    ppermute x0 -> x3, starting transfers between devices: none -> 6.33 us  [_recast_ticks(): lax.ppermute(base_arr, axis_name=axis_id, perm=tuple(((k0, k0 ^ shaped) f...]
  transfers between devices with their start and end apart: 6 -> 8, of which waited for: 6 -> 7; matrix products, arithmetic and copies ran while one was open for 5% -> 4% of each run, Pallas kernels for 0% -> 0%
where the time goes in v1:
time: 180 us; the launch traced here: 179 us
  waiting for transfers between devices  90.9 us (50%)
  blocking collectives  40.4 us (22%)
  between operations  15 us (8%)
  starting transfers between devices  14.5 us (8%)
  matrix products  11.3 us (6%)
  other arithmetic  4.4 us (2%)
  local copies, waits for them, and re-layouts  2.91 us (2%)
    ppermute x3, waiting for transfers between devices, _recast_ticks(): lax.ppermute(base_arr, axis_name=axis_id, perm=tuple(((k0, k0 ^ shaped) f...  45.1 us
    all_to_all x1, blocking collectives, local(): lax.all_to_all(send_rows, 'ctx', split_axis=0, concat_axis=0, tiled=True)  40.4 us
    all_to_all x1, waiting for transfers between devices, local(): lax.all_to_all(produced.astype(jnp.bfloat16), 'ctx', split_axis=0, concat...  35.8 us
    ppermute x3, waiting for transfers between devices, exp_swap(): return lax.ppermute(x, 'exp', perm=[(0, 1), (1, 0)])  9.3 us
    ppermute x3, starting transfers between devices, _recast_ticks(): lax.ppermute(base_arr, axis_name=axis_id, perm=tuple(((k0, k0 ^ shaped) f...  6.33 us
    ppermute x3, starting transfers between devices, exp_swap(): return lax.ppermute(x, 'exp', perm=[(0, 1), (1, 0)])  4.52 us
  transfers between devices with their start and end apart: 8, of which 7 were waited for; matrix products, arithmetic and copies ran while one was open for 4% of the time, Pallas kernels for 0%

profile of v1, /device:TPU:0, one launch (start us, length us, event | category | flops | bytes accessed | tf_op | source)
XLA Modules:
  0.0 179.3 jit_solution(166846658654228128)
XLA Ops:
  7.9 0.9 maximum_bitcast_fusion
  9.3 1.0 collective-permute-done
  10.3 0.9 broadcast_select_fusion.5
  11.3 3.0 %collective-permute-start.1 = (bf16[2,64,1024]{2,1,0:T(8,128)(2,1)S(1)}, bf16[2,64,1024]{2,1,0:T(8,128)(2,1)S(1)}, u32[]{:S(2)}, u32[]{:S(2)}) collective-permute-start(bf16[2,64,1024]{2,1,0:T(8,128)(2,1)S(1)} %pad_maximum_fusion.2), channel_id=1, source_target_pairs={{0,4},{2,6},{4,0},{6,2},{8,12},{10,14},{12,8},{14,10},{1,5},{3,7},... | collective-permute-start | bytes 786440 | tf_op jit(solution)/shard_map/ppermute | solution.py:23
  15.8 5.1 %collective-permute-done.1 = bf16[2,64,1024]{2,1,0:T(8,128)(2,1)S(1)} collective-permute-done((bf16[2,64,1024]{2,1,0:T(8,128)(2,1)S(1)}, bf16[2,64,1024]{2,1,0:T(8,128)(2,1)S(1)}, u32[]{:S(2)}, u32[]{:S(2)}) %collective-permute-start.1) | collective-permute-done | bytes 262176 | tf_op jit(solution)/shard_map/ppermute | solution.py:23
  21.0 2.8 %collective-permute-start.2 = (bf16[4,64,1024]{2,1,0:T(8,128)(2,1)S(1)}, bf16[4,64,1024]{2,1,0:T(8,128)(2,1)S(1)}, u32[]{:S(2)}, u32[]{:S(2)}) collective-permute-start(bf16[4,64,1024]{2,1,0:T(8,128)(2,1)S(1)} %pad_maximum_fusion.1), channel_id=1, source_target_pairs={{0,8},{2,10},{4,12},{6,14},{8,0},{10,2},{12,4},{14,6},{1,9},{3,11}... | collective-permute-start | bytes 1572872 | tf_op jit(solution)/shard_map/ppermute | solution.py:23
  24.0 39.0 %collective-permute-done.2 = bf16[4,64,1024]{2,1,0:T(8,128)(2,1)S(1)} collective-permute-done((bf16[4,64,1024]{2,1,0:T(8,128)(2,1)S(1)}, bf16[4,64,1024]{2,1,0:T(8,128)(2,1)S(1)}, u32[]{:S(2)}, u32[]{:S(2)}) %collective-permute-start.2) | collective-permute-done | bytes 524320 | tf_op jit(solution)/shard_map/ppermute | solution.py:23
  63.2 1.0 copy-done.1
  65.6 2.4 %fusion.38 = f32[64,2048]{1,0:T(8,128)S(1)} fusion(bf16[2048,512]{1,0:T(8,128)(2,1)} %all-gather.2.cloned.1.call-done, bf16[4,8,8,128]{3,2,1,0:T(8,128)(2,1)S(1)} %fusion.15), kind=kOutput, calls=%fused_computation.61 | convolution fusion | flops 134217728 | bytes 2686976 | tf_op jit(solution)/shard_map/tc,oc->to/dot_general | solution.py:153
  68.0 1.5 collective-permute-start.3
  70.2 3.3 %collective-permute-done.3 = bf16[32,2048]{1,0:T(8,128)(2,1)S(1)} collective-permute-done((bf16[32,2048]{1,0:T(8,128)(2,1)S(1)}, bf16[32,2048]{1,0:T(8,128)(2,1)S(1)}, u32[]{:S(2)}, u32[]{:S(2)}) %collective-permute-start.3) | collective-permute-done | bytes 131104 | tf_op jit(solution)/shard_map/ppermute | solution.py:67
  73.7 1.5 collective-permute-start.4
  75.4 3.3 %collective-permute-done.4 = bf16[32,2048]{1,0:T(8,128)(2,1)S(1)} collective-permute-done((bf16[32,2048]{1,0:T(8,128)(2,1)S(1)}, bf16[32,2048]{1,0:T(8,128)(2,1)S(1)}, u32[]{:S(2)}, u32[]{:S(2)}) %collective-permute-start.4) | collective-permute-done | bytes 131104 | tf_op jit(solution)/shard_map/ppermute | solution.py:67
  79.4 40.4 %all_to_all.10 = bf16[8,48,2048]{2,1,0:T(8,128)(2,1)S(1)} all-to-all(bf16[8,48,2048]{2,1,0:T(8,128)(2,1)S(1)} %bitcast.80), channel_id=1, replica_groups=mesh['req'=2,'ctx'=8,'exp'=2] {'ctx'}, dimensions={0} | all-to-all | bytes 3145728 | tf_op jit(solution)/shard_map/all_to_all | solution.py:171
  119.7 0.9 fusion.3
  121.1 0.9 fusion.10
  122.3 2.1 %convolution_convert_fusion = bf16[8,48,2048]{2,1,0:T(8,128)(2,1)} fusion(bf16[8,48,352]{2,1,0:T(8,128)(2,1)S(1)} %bitcast.87, bf16[1,352,2048]{2,1,0:T(8,128)(2,1)S(1)} %copy-done), kind=kOutput, calls=%fused_computation | convolution fusion | flops 554434560 | bytes 3284992 | tf_op jit(solution)/shard_map/dot_general | solution.py:63
  124.4 3.6 %all-to-all-start.1 = ((bf16[8,48,2048]{2,1,0:T(8,128)(2,1)}), bf16[8,48,2048]{2,1,0:T(8,128)(2,1)S(1)}, u32[]{:S(2)}, u32[]{:S(2)}) async-start(bf16[8,48,2048]{2,1,0:T(8,128)(2,1)} %convolution_convert_fusion), calls=%async_computation.1 | async-start | bytes 3145728 | tf_op jit(solution)/shard_map/all_to_all | solution.py:177
  128.0 1.9 %fusion.16 = bf16[1,64,512]{2,1,0:T(8,128)(2,1)} fusion(s32[512]{0:T(512)S(1)} %fusion.56, s32[64]{0:T(128)S(1)} %iota_add_fusion, bf16[512,1024]{1,0:T(8,128)(2,1)} %bitcast.82), kind=kOutput, calls=%fused_computation.18 | convolution fusion | flops 33619968 | bytes 592128 | tf_op jit(solution)/shard_map/dot_general | solution.py:129
  129.9 35.8 %all-to-all-done.1 = bf16[8,48,2048]{2,1,0:T(8,128)(2,1)S(1)} async-done(((bf16[8,48,2048]{2,1,0:T(8,128)(2,1)}), bf16[8,48,2048]{2,1,0:T(8,128)(2,1)S(1)}, u32[]{:S(2)}, u32[]{:S(2)}) %all-to-all-start.1) | async-done | bytes 1572896 | tf_op jit(solution)/shard_map/all_to_all | solution.py:177
  165.8 0.9 fusion.73
  166.7 1.5 collective-permute-start.5
  168.2 0.9 fusion.17
  169.1 2.7 %collective-permute-done.5 = bf16[32,2048]{1,0:T(8,128)(2,1)S(1)} collective-permute-done((bf16[32,2048]{1,0:T(8,128)(2,1)S(1)}, bf16[32,2048]{1,0:T(8,128)(2,1)S(1)}, u32[]{:S(2)}, u32[]{:S(2)}) %collective-permute-start.5) | collective-permute-done | bytes 131104 | tf_op jit(solution)/shard_map/ppermute | solution.py:67
  (62 shorter events, 7.0 us)
Async XLA Ops:
  7.2 115.1 %copy-start = (bf16[1,352,2048]{2,1,0:T(8,128)(2,1)S(1)}, bf16[1,352,2048]{2,1,0:T(8,128)(2,1)}, u32[]{:S(2)}) copy-start(bf16[1,352,2048]{2,1,0:T(8,128)(2,1)} %param.20) | copy-start | bytes 4325380
  7.2 7.8 %copy-start.4 = (bf16[1,64,512]{2,1,0:T(8,128)(2,1)S(1)}, bf16[1,64,512]{2,1,0:T(8,128)(2,1)}, u32[]{:S(2)}) copy-start(bf16[1,64,512]{2,1,0:T(8,128)(2,1)} %param.12) | copy-start | bytes 196612
  7.2 7.8 %copy-start.7 = (s32[1,64,4]{1,2,0:T(4,128)S(1)}, s32[1,64,4]{1,2,0:T(4,128)}, u32[]{:S(2)}) copy-start(s32[1,64,4]{1,2,0:T(4,128)} %param.21) | copy-start | bytes 3076
  7.2 58.4 %all-gather.2.cloned.1.call-start = ((), (), s32[]{:S(2)}) async-start(), calls=%async_computation.2 | async-start | bytes 2359296 | tf_op jit(solution)/shard_map/all_gather | solution.py:156
  8.8 1.5 collective-permute-start
  11.3 9.6 %collective-permute-start.1 = (bf16[2,64,1024]{2,1,0:T(8,128)(2,1)S(1)}, bf16[2,64,1024]{2,1,0:T(8,128)(2,1)S(1)}, u32[]{:S(2)}, u32[]{:S(2)}) collective-permute-start(bf16[2,64,1024]{2,1,0:T(8,128)(2,1)S(1)} %pad_maximum_fusion.2), channel_id=1, source_target_pairs={{0,4},{2,6},{4,0},{6,2},{8,12},{10,14},{12,8},{14,10},{1,5},{3,7},... | collective-permute-start | bytes 786440 | tf_op jit(solution)/shard_map/ppermute | solution.py:23
  21.0 42.0 %collective-permute-start.2 = (bf16[4,64,1024]{2,1,0:T(8,128)(2,1)S(1)}, bf16[4,64,1024]{2,1,0:T(8,128)(2,1)S(1)}, u32[]{:S(2)}, u32[]{:S(2)}) collective-permute-start(bf16[4,64,1024]{2,1,0:T(8,128)(2,1)S(1)} %pad_maximum_fusion.1), channel_id=1, source_target_pairs={{0,8},{2,10},{4,12},{6,14},{8,0},{10,2},{12,4},{14,6},{1,9},{3,11}... | collective-permute-start | bytes 1572872 | tf_op jit(solution)/shard_map/ppermute | solution.py:23
  63.2 1.0 copy-start.1
  65.6 7.8 %copy-start.3 = (bf16[1,32,2048]{2,1,0:T(8,128)(2,1)S(1)}, bf16[1,32,2048]{2,1,0:T(8,128)(2,1)}, u32[]{:S(2)}) copy-start(bf16[1,32,2048]{2,1,0:T(8,128)(2,1)} %param.15) | copy-start | bytes 393220
  65.6 8.0 %copy-start.5 = (f32[2048]{0:T(1024)S(1)}, f32[2048]{0:T(1024)}, u32[]{:S(2)}) copy-start(f32[2048]{0:T(1024)} %param.17) | copy-start | bytes 24580
  68.0 7.3 %copy-start.6 = (f32[1,64,4]{1,2,0:T(4,128)S(1)}, f32[1,64,4]{1,2,0:T(4,128)}, u32[]{:S(2)}) copy-start(f32[1,64,4]{1,2,0:T(4,128)} %param.22) | copy-start | bytes 3076
  68.0 5.4 %collective-permute-start.3 = (bf16[32,2048]{1,0:T(8,128)(2,1)S(1)}, bf16[32,2048]{1,0:T(8,128)(2,1)S(1)}, u32[]{:S(2)}, u32[]{:S(2)}) collective-permute-start(bf16[32,2048]{1,0:T(8,128)(2,1)S(1)} %select_convert_fusion.1), channel_id=1, source_target_pairs={{0,1},{1,0},{2,3},{3,2},{4,5},{5,4},{6,7},{7,6},{8,9},{9,8},{10,11... | collective-permute-start | bytes 393224 | tf_op jit(solution)/shard_map/ppermute | solution.py:67
  73.7 5.0 %collective-permute-start.4 = (bf16[32,2048]{1,0:T(8,128)(2,1)S(1)}, bf16[32,2048]{1,0:T(8,128)(2,1)S(1)}, u32[]{:S(2)}, u32[]{:S(2)}) collective-permute-start(bf16[32,2048]{1,0:T(8,128)(2,1)S(1)} %fusion.22), channel_id=1, source_target_pairs={{0,1},{1,0},{2,3},{3,2},{4,5},{5,4},{6,7},{7,6},{8,9},{9,8},{10,11... | collective-permute-start | bytes 393224 | tf_op jit(solution)/shard_map/ppermute | solution.py:67
  79.3 40.4 %copy-start.8 = (bf16[1,2048,352]{1,2,0:T(8,128)(2,1)S(1)}, bf16[1,2048,352]{1,2,0:T(8,128)(2,1)}, u32[]{:S(2)}) copy-start(bf16[1,2048,352]{1,2,0:T(8,128)(2,1)} %param.18) | copy-start | bytes 4325380
  119.7 1.4 copy-start.9
  124.4 41.3 %all-to-all-start.1 = ((bf16[8,48,2048]{2,1,0:T(8,128)(2,1)}), bf16[8,48,2048]{2,1,0:T(8,128)(2,1)S(1)}, u32[]{:S(2)}, u32[]{:S(2)}) async-start(bf16[8,48,2048]{2,1,0:T(8,128)(2,1)} %convolution_convert_fusion), calls=%async_computation.1 | async-start | bytes 3145728 | tf_op jit(solution)/shard_map/all_to_all | solution.py:177
  165.8 2.4 %copy-start.2 = (bf16[8,64,1024]{2,1,0:T(8,128)(2,1)S(1)}, bf16[8,64,1024]{2,1,0:T(8,128)(2,1)}, u32[]{:S(2)}) copy-start(bf16[8,64,1024]{2,1,0:T(8,128)(2,1)} %copy-done.1) | copy-start | bytes 3145732
  166.7 5.1 %collective-permute-start.5 = (bf16[32,2048]{1,0:T(8,128)(2,1)S(1)}, bf16[32,2048]{1,0:T(8,128)(2,1)S(1)}, u32[]{:S(2)}, u32[]{:S(2)}) collective-permute-start(bf16[32,2048]{1,0:T(8,128)(2,1)S(1)} %select_convert_fusion), channel_id=1, source_target_pairs={{0,1},{1,0},{2,3},{3,2},{4,5},{5,4},{6,7},{7,6},{8,9},{9,8},{10,11... | collective-permute-start | bytes 393224 | tf_op jit(solution)/shard_map/ppermute | solution.py:67
Sparse Core Ops, SparseCore 0:
  9.6 51.8 all-gather.1
